TPU v7x, 256 devices: a whole 4x4x8 slice. The times are simulated.
256 devices in a mesh: grp: 32 (over x, z), shard: 8 (over y, core).
Axes of the slice: x: 4, y: 4, z: 8, core: 2. Of those that a mesh axis runs over, the one named last changes fastest.
Arguments:
- layer_inputs: bfloat16 [131072, 1600], P(('grp', 'shard')), may hold values from -6 to 6
- cotangents: bfloat16 [131072, 1600], P(('grp', 'shard')), may hold values from -0.25 to 0.25
- weight: bfloat16 [1600, 1600], P('shard'), may hold values from -0.15625 to 0.15625
- error_state: float32 [32, 1600, 1600], P('grp', 'shard'), may hold values from -6 to 6
- momentum: float32 [1600, 1600], P('shard'), may hold values from -0.75 to 0.75
- bias_momentum: float32 [1600], replicated, may hold values from -6 to 6
- start_basis: float32 [1600, 32], replicated, may hold values from -6 to 6
- next_inputs: bfloat16 [131072, 1600], P(('grp', 'shard')), may hold values from -6 to 6
Outputs:
- next_outputs: bfloat16 [131072, 1600], P(('grp', 'shard'))
- new_error: float32 [32, 1600, 1600], P('grp', 'shard')
- new_momentum: float32 [1600, 1600], P('shard')
- new_bias_momentum: float32 [1600], replicated
All inputs are finite; a program needn't handle non-finite values.
Results may differ from a plain program's by a relative error of at most 0.015.
Values may be sent and summed in bfloat16 or wider, within the bound.
No kernel may reach another device: no remote copies, remote signals or barrier semaphores. Data moves between devices by JAX's collectives and lax.ppermute only.
A program may use at most 128 MiB of HBM per device.

v0:
```python
import jax
import jax.numpy as jnp
from jax import lax
from jax.sharding import PartitionSpec as P

momentum_decay = 0.9
learn_rate = 0.1


def shards(
    layer_inputs, cotangents, weight, error_state, momentum, bias_momentum, start_basis, next_inputs
):
    highest = lax.Precision.HIGHEST
    group_count = lax.axis_size("grp")
    columns = layer_inputs
    gradient = lax.psum_scatter(
        lax.dot_general(
            columns, cotangents, (((0,), (0,)), ((), ())), preferred_element_type=jnp.float32
        ).astype(jnp.bfloat16),
        "shard",
        scatter_dimension=0,
        tiled=True,
    ).astype(jnp.float32)
    column_sums = lax.psum(jnp.sum(cotangents, axis=0, dtype=jnp.float32), ("grp", "shard"))
    corrected = gradient + error_state[0]
    basis = start_basis
    ortho = start_basis
    for round_index in range(2):
        local_factor = jnp.dot(corrected, basis, precision=highest)
        own_rows = lax.psum(local_factor, "grp")
        gram = lax.psum(jnp.dot(own_rows.T, own_rows, precision=highest), "shard")
        lower_factor = jnp.linalg.cholesky(gram)
        ortho = jax.scipy.linalg.solve_triangular(lower_factor, own_rows.T, lower=True).T
        partial_basis = lax.dot_general(
            corrected, ortho, (((0,), (0,)), ((), ())), precision=highest
        )
        summed = lax.psum(partial_basis, ("grp", "shard"))
        basis = summed / group_count
    approx = jnp.dot(ortho, basis.T, precision=highest)
    new_error = (corrected - approx)[None, :, :]
    new_momentum = momentum_decay * momentum + approx
    new_bias_momentum = momentum_decay * bias_momentum + column_sums / group_count
    new_weight = (weight.astype(jnp.float32) - learn_rate * new_momentum).astype(jnp.bfloat16)
    columns = next_inputs
    projected = jnp.dot(
        columns,
        lax.all_gather(new_weight, "shard", axis=0, tiled=True),
        preferred_element_type=jnp.float32,
    )
    return (projected.astype(jnp.bfloat16), new_error, new_momentum, new_bias_momentum)


def solution(mesh):
    placed = (
        P(("grp", "shard"), None),
        P(("grp", "shard"), None),
        P("shard", None),
        P("grp", "shard", None),
        P("shard", None),
        P(),
        P(),
        P(("grp", "shard"), None),
    )
    return jax.shard_map(
        shards,
        mesh=mesh,
        in_specs=placed,
        out_specs=(P(("grp", "shard"), None), P("grp", "shard", None), P("shard", None), P()),
        check_vma=False,
    )
```

profile of v0, /device:TPU:1, one launch (start us, length us, event | category | flops | bytes accessed | tf_op | source)
XLA Modules:
  0.0 1017.4 jit_solution(5363052511592432300)
XLA Ops:
  7.2 0.0 copy-start
  7.2 0.0 reduce-scatter.4.cloned.1.call-start
  7.2 1.4 copy-done
  8.6 6.3 convolution_convert_fusion
  14.9 0.0 copy-start.1
  14.9 0.0 copy-start.2
  14.9 0.0 reduce-scatter.4.cloned.1.call-update
  15.0 0.0 all-reduce.4.cloned.1.call-start
  15.0 50.3 %reduce-scatter.4.cloned.1.call-done = bf16[200,1600]{1,0:T(8,128)(2,1)} async-done(((bf16[1600,1600]{1,0:T(8,128)(2,1)}), bf16[200,1600]{1,0:T(8,128)(2,1)}) %reduce-scatter.4.cloned.1.call-update) | async-done | bytes 640016
  65.3 0.0 copy-done.1
  65.3 0.0 copy-done.2
  65.3 2.4 fusion.23
  67.8 115.4 %psum.49 = f32[200,32]{0,1:T(8,128)S(1)} all-reduce(f32[200,32]{0,1:T(8,128)S(1)} %fusion.23), channel_id=1, replica_groups=mesh['grp'=32,'shard'=8] {'grp'}, use_global_device_ids=true, to_apply=%region_1.0 | all-reduce | flops 6400 | bytes 51200 | tf_op jit(solution)/shard_map/psum | solution.py:30
  183.2 0.2 fusion.26
  183.4 51.6 %psum.50 = f32[32,32]{0,1:T(8,128)S(1)} all-reduce(f32[32,32]{0,1:T(8,128)S(1)} %fusion.26), channel_id=1, replica_groups=mesh['grp'=32,'shard'=8] {'shard'}, use_global_device_ids=true, to_apply=%region_2.0 | all-reduce | flops 1024 | bytes 8192 | tf_op jit(solution)/shard_map/psum | solution.py:31
  234.9 0.1 copy.17
  235.0 2.9 cholesky.44
  238.0 0.6 compare_reduce_fusion.1
  238.6 0.7 fusion.11
  239.3 2.4 custom-call.6
  241.7 0.2 fusion.9
  242.0 4.8 fusion.22
  246.7 0.0 all-reduce.4.cloned.1.call-update
  246.8 0.0 all-reduce.6.cloned.1.call-start
  246.8 248.4 %all-reduce.4.cloned.1.call-done = f32[1600,32]{1,0:T(8,128)} async-done(((f32[1600,32]{1,0:T(8,128)}), f32[1600,32]{1,0:T(8,128)}) %all-reduce.4.cloned.1.call-update) | async-done | bytes 204816 | tf_op jit(solution)/shard_map/psum | solution.py:37
  495.2 2.9 fusion.3
  498.1 114.1 %psum.52 = f32[200,32]{0,1:T(8,128)S(1)} all-reduce(f32[200,32]{0,1:T(8,128)S(1)} %fusion.3), channel_id=1, replica_groups=mesh['grp'=32,'shard'=8] {'grp'}, use_global_device_ids=true, to_apply=%region_6.0 | all-reduce | flops 6400 | bytes 51200 | tf_op jit(solution)/shard_map/psum | solution.py:30
  612.2 0.2 fusion.27
  612.4 46.1 %psum.53 = f32[32,32]{0,1:T(8,128)S(1)} all-reduce(f32[32,32]{0,1:T(8,128)S(1)} %fusion.27), channel_id=1, replica_groups=mesh['grp'=32,'shard'=8] {'shard'}, use_global_device_ids=true, to_apply=%region_7.0 | all-reduce | flops 1024 | bytes 8192 | tf_op jit(solution)/shard_map/psum | solution.py:31
  658.5 0.1 copy.19
  658.6 2.9 cholesky.55
  661.6 0.6 compare_reduce_fusion
  662.2 0.7 fusion.12
  662.9 2.4 custom-call.7
  665.3 0.2 fusion.7
  665.5 4.8 fusion.21
  670.3 0.0 all-reduce.6.cloned.1.call-update
  670.4 0.0 all-gather.2.cloned.1.call-start
  670.4 248.4 %all-reduce.6.cloned.1.call-done = f32[1600,32]{1,0:T(8,128)} async-done(((f32[1600,32]{1,0:T(8,128)}), f32[1600,32]{1,0:T(8,128)}) %all-reduce.6.cloned.1.call-update) | async-done | bytes 204816 | tf_op jit(solution)/shard_map/psum | solution.py:37
  918.8 5.3 subtract_convert_fusion
  924.0 0.0 copy-start.3
  924.1 0.0 all-gather.2.cloned.1.call-update
  924.1 1.7 convert_reduce_fusion
  925.8 77.1 %psum.55 = f32[1600]{0:T(1024)S(1)} all-reduce(f32[1600]{0:T(1024)S(1)} %convert_reduce_fusion), channel_id=1, replica_groups=mesh['grp'=32,'shard'=8] {'grp','shard'}, use_global_device_ids=true, to_apply=%region_10.13 | all-reduce | flops 1600 | bytes 12800 | tf_op jit(solution)/shard_map/psum | solution.py:24
  1002.9 0.0 copy-done.3
  1002.9 0.6 multiply_add_fusion.1
  1003.5 0.0 all-gather.2.cloned.1.call-done
  1003.5 7.4 fusion
  (4 shorter events, 0.1 us)
Async XLA Ops:
  7.2 1.4 copy-start
  7.2 58.1 %reduce-scatter.4.cloned.1.call-start = ((), (), s32[]{:S(2)}) async-start(), calls=%async_computation.4 | async-start | bytes 5990400
  14.9 50.4 %copy-start.1 = (f32[1,200,1600]{2,1,0:T(8,128)S(1)}, f32[1,200,1600]{2,1,0:T(8,128)}, u32[]{:S(2)}) copy-start(f32[1,200,1600]{2,1,0:T(8,128)} %param.14) | copy-start | bytes 3840004
  14.9 50.4 %copy-start.2 = (f32[1600,32]{0,1:T(8,128)S(1)}, f32[1600,32]{0,1:T(8,128)}, u32[]{:S(2)}) copy-start(f32[1600,32]{0,1:T(8,128)} %param.17) | copy-start | bytes 614404
  15.0 480.3 %all-reduce.4.cloned.1.call-start = ((), (), s32[]{:S(2)}) async-start(), calls=%async_computation.1 | async-start | bytes 1638400 | tf_op jit(solution)/shard_map/psum | solution.py:37
  246.8 672.0 %all-reduce.6.cloned.1.call-start = ((), (), s32[]{:S(2)}) async-start(), calls=%async_computation.2 | async-start | bytes 1638400 | tf_op jit(solution)/shard_map/psum | solution.py:37
  670.4 333.1 %all-gather.2.cloned.1.call-start = ((), (), s32[]{:S(2)}) async-start(), calls=%async_computation.3 | async-start | bytes 5990400 | tf_op jit(solution)/shard_map/all_gather | solution.py:47
  924.0 78.8 %copy-start.3 = (f32[1600]{0:T(1024)S(1)}, f32[1600]{0:T(1024)}, u32[]{:S(2)}) copy-start(f32[1600]{0:T(1024)} %param.16) | copy-start | bytes 19204
Sparse Core Ops, SparseCore 0:
  15.1 50.1 reduce-scatter.3
  246.9 248.2 all-reduce.3
  670.5 248.2 all-reduce.5
  924.2 38.9 all-gather.1
where the time goes:
time: 1020 us
  waiting for transfers between devices  547 us (54%)
  blocking collectives  404 us (40%)
  matrix products  34.6 us (3%)
  other arithmetic  15.7 us (2%)
  between operations  13.8 us (1%)
    psum x2, waiting for transfers between devices, shards(): summed = lax.psum(partial_basis, ('grp', 'shard'))  497 us
    psum x2, blocking collectives, shards(): own_rows = lax.psum(local_factor, 'grp')  230 us
    psum x2, blocking collectives, shards(): gram = lax.psum(jnp.dot(own_rows.T, own_rows, precision=highest), 'shard')  97.7 us
    psum x1, blocking collectives, shards(): lax.psum(jnp.sum(cotangents, axis=0, dtype=jnp.float32), ('grp', 'shard'))  77.1 us
    unnamed x5, waiting for transfers between devices  50.4 us
  transfers between devices with their start and end apart: 4, of which 3 were waited for; matrix products, arithmetic and copies ran while one was open for 0% of the time, Pallas kernels for 0%

commit v1 on v0

--- a/solution.py
+++ b/solution.py
@@ -34,7 +34,7 @@
         partial_basis = lax.dot_general(
             corrected, ortho, (((0,), (0,)), ((), ())), precision=highest
         )
-        summed = lax.psum(partial_basis, ("grp", "shard"))
+        summed = jnp.sum(lax.all_gather(partial_basis, ("grp", "shard")), axis=0)
         basis = summed / group_count
     approx = jnp.dot(ortho, basis.T, precision=highest)
     new_error = (corrected - approx)[None, :, :]

time: 1020 us -> 914 us (0.90)
  waiting for transfers between devices: 547 us -> 416 us
  other arithmetic: 15.7 us -> 50.5 us
    psum x2 -> x0, waiting for transfers between devices: 497 us -> none  [shards(): summed = lax.psum(partial_basis, ('grp', 'shard'))]
    all_gather x0 -> x2, waiting for transfers between devices: none -> 366 us  [shards(): summed = jnp.sum(lax.all_gather(partial_basis, ('grp', 'shard')), axis=0)]
    reduce_sum x0 -> x2, other arithmetic: none -> 34.7 us  [shards(): summed = jnp.sum(lax.all_gather(partial_basis, ('grp', 'shard')), axis=0)]
where the time goes in v1:
time: 914 us; the launch traced here: 913 us
  waiting for transfers between devices  416 us (46%)
  blocking collectives  404 us (44%)
  other arithmetic  50.5 us (6%)
  matrix products  26.4 us (3%)
  between operations  13.9 us (2%)
    all_gather x2, waiting for transfers between devices, shards(): summed = jnp.sum(lax.all_gather(partial_basis, ('grp', 'shard')), axis=0)  366 us
    psum x2, blocking collectives, shards(): own_rows = lax.psum(local_factor, 'grp')  229 us
    psum x2, blocking collectives, shards(): gram = lax.psum(jnp.dot(own_rows.T, own_rows, precision=highest), 'shard')  99.7 us
    psum x1, blocking collectives, shards(): lax.psum(jnp.sum(cotangents, axis=0, dtype=jnp.float32), ('grp', 'shard'))  75.8 us
    unnamed x5, waiting for transfers between devices  50.5 us
    reduce_sum x2, other arithmetic, shards(): summed = jnp.sum(lax.all_gather(partial_basis, ('grp', 'shard')), axis=0)  34.7 us
  transfers between devices with their start and end apart: 4, of which 3 were waited for; matrix products, arithmetic and copies ran while one was open for 0% of the time, Pallas kernels for 0%

profile of v1, /device:TPU:1, one launch (start us, length us, event | category | flops | bytes accessed | tf_op | source)
XLA Modules:
  0.0 913.3 jit_solution(6676171794267850291)
XLA Ops:
  7.2 0.0 copy-start
  7.2 0.0 reduce-scatter.4.cloned.1.call-start
  7.2 1.4 copy-done
  8.6 6.3 convolution_convert_fusion
  14.9 0.0 reduce-scatter.4.cloned.1.call-update
  15.0 0.0 all-gather.10.cloned.1.call-start
  15.0 50.4 %reduce-scatter.4.cloned.1.call-done = bf16[200,1600]{1,0:T(8,128)(2,1)} async-done(((bf16[1600,1600]{1,0:T(8,128)(2,1)}), bf16[200,1600]{1,0:T(8,128)(2,1)}) %reduce-scatter.4.cloned.1.call-update) | async-done | bytes 640016
  65.4 0.0 copy-done.2
  65.4 0.0 copy-done.6
  65.4 2.5 fusion.21
  67.9 115.0 %psum.35 = f32[200,32]{0,1:T(8,128)S(1)} all-reduce(f32[200,32]{0,1:T(8,128)S(1)} %fusion.21), channel_id=1, replica_groups=mesh['grp'=32,'shard'=8] {'grp'}, use_global_device_ids=true, to_apply=%region_1.0 | all-reduce | flops 6400 | bytes 51200 | tf_op jit(solution)/shard_map/psum | solution.py:30
  183.0 0.2 fusion.24
  183.1 52.0 %psum.36 = f32[32,32]{0,1:T(8,128)S(1)} all-reduce(f32[32,32]{0,1:T(8,128)S(1)} %fusion.24), channel_id=1, replica_groups=mesh['grp'=32,'shard'=8] {'shard'}, use_global_device_ids=true, to_apply=%region_2.0 | all-reduce | flops 1024 | bytes 8192 | tf_op jit(solution)/shard_map/psum | solution.py:31
  235.1 0.1 copy.17
  235.2 2.9 cholesky.44
  238.2 0.6 compare_reduce_fusion.1
  238.8 0.7 fusion.11
  239.5 2.4 custom-call.6
  241.9 0.2 fusion.9
  242.2 1.7 convolution_bitcast_fusion.1
  243.9 0.0 all-gather.10.cloned.1.call-update
  243.9 0.0 all-gather.12.cloned.1.call-start
  243.9 182.8 %all-gather.10.cloned.1.call-done = f32[256,1600,32]{1,2,0:T(8,128)} async-done(((f32[1,1600,32]{1,2,0:T(8,128)}), f32[256,1600,32]{1,2,0:T(8,128)}) %all-gather.10.cloned.1.call-update) | async-done | bytes 52428816 | tf_op jit(solution)/shard_map/all_gather | solution.py:37
  426.7 17.4 %reduce_sum.27 = f32[1600,32]{0,1:T(8,128)S(1)} reduce(f32[256,1600,32]{1,2,0:T(8,128)} %all-gather.10.cloned.1.call-done, f32[]{:T(128)} %constant.41.clone.1), dimensions={0}, to_apply=%region_5.0 | reduce | flops 13056000 | bytes 52633604 | tf_op jit(solution)/shard_map/reduce_sum | solution.py:37
  444.1 1.4 fusion.3
  445.5 113.7 %psum.37 = f32[200,32]{0,1:T(8,128)S(1)} all-reduce(f32[200,32]{0,1:T(8,128)S(1)} %fusion.3), channel_id=1, replica_groups=mesh['grp'=32,'shard'=8] {'grp'}, use_global_device_ids=true, to_apply=%region_6.0 | all-reduce | flops 6400 | bytes 51200 | tf_op jit(solution)/shard_map/psum | solution.py:30
  559.2 0.2 fusion.25
  559.4 47.7 %psum.38 = f32[32,32]{0,1:T(8,128)S(1)} all-reduce(f32[32,32]{0,1:T(8,128)S(1)} %fusion.25), channel_id=1, replica_groups=mesh['grp'=32,'shard'=8] {'shard'}, use_global_device_ids=true, to_apply=%region_7.0 | all-reduce | flops 1024 | bytes 8192 | tf_op jit(solution)/shard_map/psum | solution.py:31
  607.1 0.1 copy.19
  607.1 2.9 cholesky.55
  610.1 0.6 compare_reduce_fusion
  610.7 0.7 fusion.12
  611.4 2.4 custom-call.7
  613.8 0.2 fusion.7
  614.1 0.6 copy-done.5
  614.7 1.7 convolution_bitcast_fusion
  616.4 0.0 all-gather.12.cloned.1.call-update
  616.4 0.0 copy-start.4
  616.4 0.0 all-gather.8.cloned.1.call-start
  616.5 182.8 %all-gather.12.cloned.1.call-done = f32[256,1600,32]{1,2,0:T(8,128)} async-done(((f32[1,1600,32]{1,2,0:T(8,128)}), f32[256,1600,32]{1,2,0:T(8,128)}) %all-gather.12.cloned.1.call-update) | async-done | bytes 52428816 | tf_op jit(solution)/shard_map/all_gather | solution.py:37
  799.3 17.4 %reduce_sum.28 = f32[1600,32]{0,1:T(8,128)S(1)} reduce(f32[256,1600,32]{1,2,0:T(8,128)} %all-gather.12.cloned.1.call-done, f32[]{:T(128)} %constant.41.clone.1), dimensions={0}, to_apply=%region_8.0 | reduce | flops 13056000 | bytes 52633604 | tf_op jit(solution)/shard_map/reduce_sum | solution.py:37
  816.6 0.0 copy-done.4
  816.6 4.4 subtract_convert_fusion
  821.0 0.0 all-gather.8.cloned.1.call-update
  821.1 1.7 convert_reduce_fusion
  822.8 75.8 %psum.39 = f32[1600]{0:T(1024)S(1)} all-reduce(f32[1600]{0:T(1024)S(1)} %convert_reduce_fusion), channel_id=1, replica_groups=mesh['grp'=32,'shard'=8] {'grp','shard'}, use_global_device_ids=true, to_apply=%region_10.13 | all-reduce | flops 1600 | bytes 12800 | tf_op jit(solution)/shard_map/psum | solution.py:24
  898.7 0.6 multiply_add_fusion.1
  899.3 7.5 fusion
  (14 shorter events, 0.1 us)
Async XLA Ops:
  7.2 1.4 copy-start
  7.2 58.2 %reduce-scatter.4.cloned.1.call-start = ((), (), s32[]{:S(2)}) async-start(), calls=%async_computation.4 | async-start | bytes 5990400
  14.9 50.5 %copy-start.2 = (f32[1,200,1600]{2,1,0:T(8,128)S(1)}, f32[1,200,1600]{2,1,0:T(8,128)}, u32[]{:S(2)}) copy-start(f32[1,200,1600]{2,1,0:T(8,128)} %param.14) | copy-start | bytes 3840004
  14.9 50.5 %copy-start.6 = (f32[1600,32]{0,1:T(8,128)S(1)}, f32[1600,32]{0,1:T(8,128)}, u32[]{:S(2)}) copy-start(f32[1600,32]{0,1:T(8,128)} %param.17) | copy-start | bytes 614404
  15.0 411.8 %all-gather.10.cloned.1.call-start = ((), (), s32[]{:S(2)}) async-start(), calls=%async_computation.2 | async-start | bytes 54738944 | tf_op jit(solution)/shard_map/all_gather | solution.py:37
  65.4 176.7 %copy-start.3 = (bf16[200,1600]{1,0:T(8,128)(2,1)S(1)}, bf16[200,1600]{1,0:T(8,128)(2,1)}, u32[]{:S(2)}) copy-start(bf16[200,1600]{1,0:T(8,128)(2,1)} %reduce-scatter.4.cloned.1.call-done) | copy-start | bytes 1920004
  243.9 555.4 %all-gather.12.cloned.1.call-start = ((), (), s32[]{:S(2)}) async-start(), calls=%async_computation.3 | async-start | bytes 54738944 | tf_op jit(solution)/shard_map/all_gather | solution.py:37
  614.1 0.6 copy-start.5
  616.4 200.2 %copy-start.4 = (f32[200,1600]{1,0:T(8,128)S(1)}, f32[200,1600]{1,0:T(8,128)}, u32[]{:S(2)}) copy-start(f32[200,1600]{1,0:T(8,128)} %param.15) | copy-start | bytes 3840004
  616.4 282.8 %all-gather.8.cloned.1.call-start = ((), (), s32[]{:S(2)}) async-start(), calls=%async_computation.1 | async-start | bytes 5990400 | tf_op jit(solution)/shard_map/all_gather | solution.py:47
  821.0 77.6 %copy-start.7 = (f32[1600]{0:T(1024)S(1)}, f32[1600]{0:T(1024)}, u32[]{:S(2)}) copy-start(f32[1600]{0:T(1024)} %param.16) | copy-start | bytes 19204
  899.3 7.5 copy-start.1
Sparse Core Ops, SparseCore 0:
  15.1 50.2 reduce-scatter.3
  244.0 182.6 all-gather.9
  616.5 182.6 all-gather.11
  821.2 36.8 all-gather.7
